TPU v7x, 32 devices: a whole 2x2x4 slice. The times are simulated.
32 devices in a mesh: row: 4 (over y, x), col: 8 (over z, core).
Axes of the slice: x: 2, y: 2, z: 4, core: 2. Of those that a mesh axis runs over, the one named last changes fastest.
Arguments:
- sensitivity: bfloat16 [8192, 8, 4096], P('row', None, 'col'), may hold values from -0.25 to 0.25
- sample_weight: float32 [8192], P('row'), may hold values from 0.2 to 5
- pattern: int32 [16, 8, 8], P('row', None, 'col'), may hold values 0 or 1
- prior: float32 [2048], P('row'), may hold values from 0.5 to 5
Outputs:
- factored_band: float32 [2048, 8, 4096], P('row', None, 'col')
Inputs may be any that keep to these rules, and one draw needn't show every extreme that they name: pattern holds only 0 and 1.
All inputs are finite; a program needn't handle non-finite values. No bound on the sum of `pattern` on one device may be relied on, other than what follows from the above.
Results may differ from a plain program's by a relative error of at most 0.0028.
Values may be sent and summed in bfloat16 or wider, within the bound.
No kernel may reach another device: no remote copies, remote signals or barrier semaphores. Data moves between devices by JAX's collectives and lax.ppermute only.
A program may use at most 128 MiB of HBM per device.

v0:
```python
import jax
import jax.numpy as jnp
from jax import lax
from jax.sharding import PartitionSpec as P


def spread(value, axis, root):
    mine = lax.axis_index(axis) == root
    return lax.psum(jnp.where(mine, value, jnp.zeros_like(value)), axis)


def body(sensitivity, sample_weight, pattern, prior):
    rows_here = sensitivity.shape[0]
    cycles = sensitivity.shape[1]
    tile = sensitivity.shape[2]
    blocks = pattern.shape[0]
    widths = cycles * tile
    mask_blocks = pattern.astype(jnp.bfloat16)[:, None, :, :]
    masked = (sensitivity.reshape(blocks, tile, cycles, tile) * mask_blocks).reshape(
        rows_here, widths
    )
    weighted = (sample_weight[:, None] * masked.astype(jnp.float32)).astype(jnp.bfloat16)
    first_tile = masked[:, :tile]
    row_count = lax.axis_size("row")
    band_parts = []
    for owner in range(row_count):
        band_parts.append(spread(first_tile, "col", owner))
    band = jnp.concatenate(band_parts, axis=1)
    fisher = lax.psum_scatter(
        jnp.einsum("sb,sc->bc", band, weighted, preferred_element_type=jnp.float32),
        "row",
        scatter_dimension=0,
        tiled=True,
    )
    on_diagonal = (lax.axis_index("col") == lax.axis_index("row")).astype(jnp.float32)
    identity = jnp.eye(tile, dtype=jnp.float32)
    fisher = fisher.at[:, :tile].add(on_diagonal * identity * prior[None, :])
    corner = spread(fisher[:, :tile], "col", 0)
    lower = jnp.linalg.cholesky(corner)
    local_solved = jax.scipy.linalg.solve_triangular(lower, fisher, lower=True)
    solved = spread(local_solved, "row", 0)
    solved_mine = spread(solved[:, :tile], "col", lax.axis_index("row"))
    updated = fisher - jnp.dot(solved_mine.T, solved, precision=lax.Precision.HIGHEST)
    result = jnp.where(lax.axis_index("row") == 0, solved, updated)
    return result.reshape(tile, cycles, tile)


def solution(mesh):
    return jax.shard_map(
        body,
        mesh=mesh,
        in_specs=(P("row", None, "col"), P("row"), P("row", None, "col"), P("row")),
        out_specs=P("row", None, "col"),
        check_vma=False,
    )
```

profile of v0, /device:TPU:0, one launch (start us, length us, event | category | flops | bytes accessed | tf_op | source)
XLA Modules:
  0.0 1079.7 jit_solution(16015957942171374049)
XLA Ops:
  9.0 6.3 copy.29
  15.2 12.2 %copy.28 = bf16[256,8,8,512]{3,1,2,0:T(8,128)(2,1)S(1)} copy(bf16[256,8,8,512]{3,2,1,0:T(8,128)(2,1)} %bitcast.61) | data formatting | bytes 33554432
  27.4 9.2 mul.38
  36.6 5.1 broadcast_select_fusion.3
  42.0 178.2 %all-reduce.13.cloned.1.call-done = (bf16[2048,512]{1,0:T(8,128)(2,1)}, bf16[2048,512]{1,0:T(8,128)(2,1)}, bf16[2048,512]{1,0:T(8,128)(2,1)}, bf16[2048,512]{1,0:T(8,128)(2,1)}) async-done(((bf16[2048,512]{1,0:T(8,128)(2,1)}, bf16[2048,512]{1,0:T(8,128)(2,1)}, bf16[2048,512]{1,0:T(8,128)(2,1)}, bf16[2048,512]{1,0:T(8,128)(2,1)}), (bf16[2048,512]{1,0:T(8,128)(2,1)}, bf16[2048,512]{1,0:T(8,128)(2,1)}, ...) | async-done | bytes 8388624 | tf_op jit(solution)/shard_map/psum | solution.py:9
  220.2 43.8 %fusion = f32[2048,4096]{0,1:T(8,128)} fusion(bf16[2048,4096]{1,0:T(8,128)(2,1)} %mul.38, f32[2048]{0:T(1024)S(1)} %copy-done.6, bf16[2048,512]{1,0:T(8,128)(2,1)} %get-tuple-element.37, bf16[2048,512]{1,0:T(8,128)(2,1)} %get-tuple-element.38, bf16[2048,512]{1,0:T(8,128)(2,1)} %get-tuple-element.39, bf16[2048,512]{1,0:T(8,128)(2,1)} %get-tuple-element.40), kind=kOutput, calls=%fused_computation.3 | convolution fusion | flops 34418458624 | bytes 58728448 | tf_op jit(solution)/shard_map/sb,sc->bc/dot_general | solution.py:30
  264.8 288.1 %reduce-scatter.2.cloned.1.call-done = f32[512,4096]{0,1:T(8,128)} async-done(((f32[2048,4096]{0,1:T(8,128)}), f32[512,4096]{0,1:T(8,128)}) %reduce-scatter.2.cloned.1.call-update) | async-done | bytes 8388624 | tf_op jit(solution)/shard_map/reduce_scatter | solution.py:29
  552.9 3.4 fusion.25
  556.8 59.0 %all-reduce.7.cloned.1.call-done = f32[512,512]{0,1:T(8,128)} async-done(((f32[512,512]{0,1:T(8,128)}), f32[512,512]{0,1:T(8,128)}) %all-reduce.7.cloned.1.call-update) | async-done | bytes 1048592 | tf_op jit(solution)/shard_map/psum | solution.py:9
  617.7 11.7 %cholesky.103 = f32[128,128]{1,0:T(8,128)S(1)} custom-call(f32[128,128]{1,0:T(8,128)S(1)} %cholesky.263), custom_call_target="Cholesky" | custom-call | tf_op jit(solution)/shard_map/jit(cholesky)/cholesky | solution.py:39
  629.4 9.8 custom-call.31
  639.9 11.7 %cholesky.215 = f32[128,128]{1,0:T(8,128)S(1)} custom-call(f32[128,128]{1,0:T(8,128)S(1)} %cholesky.267), custom_call_target="Cholesky" | custom-call | tf_op jit(solution)/shard_map/jit(cholesky)/cholesky | solution.py:39
  652.0 10.0 custom-call.32
  663.0 11.7 %cholesky.236 = f32[128,128]{1,0:T(8,128)S(1)} custom-call(f32[128,128]{1,0:T(8,128)S(1)} %cholesky.272), custom_call_target="Cholesky" | custom-call | tf_op jit(solution)/shard_map/jit(cholesky)/cholesky | solution.py:39
  674.9 9.8 custom-call.33
  685.5 12.1 %cholesky.253 = f32[128,128]{1,0:T(8,128)S(1)} custom-call(f32[128,128]{1,0:T(8,128)S(1)} %convolution_subtract_fusion.4), custom_call_target="Cholesky" | custom-call | tf_op jit(solution)/shard_map/jit(cholesky)/cholesky | solution.py:39
  702.5 11.3 %while.2 = (s32[]{:T(128)}, f32[512,512]{0,1:T(8,128)S(1)}, s32[4,2]{0,1:T(2,128)S(1)}, f32[4,128,128]{2,1,0:T(8,128)}, s32[]{:T(128)}) while((s32[]{:T(128)}, f32[512,512]{0,1:T(8,128)S(1)}, s32[4,2]{0,1:T(2,128)S(1)}, f32[4,128,128]{2,1,0:T(8,128)}, s32[]{:T(128)}) %tuple.32), condition=%wide.while_cond.1, body=%wide.while_body.1.sunk | while | flops 2 | bytes 393829 | solution.py:40
  713.8 40.1 %custom-call.34 = f32[4,128,128]{1,2,0:T(8,128)S(1)} custom-call(f32[4,128,128]{2,1,0:T(8,128)} %get-tuple-element.24), custom_call_target="InvertDiagBlocksLowerTriangular" | custom-call | tf_op jit(solution)/shard_map/jit(_solve_triangular)/triangular_solve | solution.py:40
  753.9 3.5 fusion.21
  757.4 5.1 convolution_subtract_fusion.1
  764.6 9.7 convolution_subtract_fusion
  774.2 2.0 fusion.35
  777.6 12.9 %fusion.15 = f32[128,4096]{0,1:T(8,128)} fusion(f32[128,4096]{1,0:T(8,128)S(1)} %fusion.35, f32[128,4096]{1,0:T(8,128)S(1)} %fusion.37, f32[128,4096]{1,0:T(8,128)S(1)} %fusion.21, f32[512,4096]{0,1:T(8,128)} %get-tuple-element.48, f32[512,512]{0,1:T(8,128)S(1)} %get-tuple-element.129), kind=kOutput, calls=%fused_computation.22 | convolution fusion | flops 2419589120 | bytes 10682368 | tf_op jit(solution)/shard_map/jit(_solve_triangular)/triangular_solve | solution.py:40
  790.4 2.9 copy.17
  793.4 2.9 copy.16
  798.1 3.5 fusion.34
  801.7 5.4 maximum_select_fusion
  807.1 171.2 %all-reduce.9.cloned.1.call-done = f32[512,4096]{0,1:T(8,128)} async-done(((f32[512,4096]{0,1:T(8,128)}), f32[512,4096]{0,1:T(8,128)}) %all-reduce.9.cloned.1.call-update) | async-done | bytes 8388624 | tf_op jit(solution)/shard_map/psum | solution.py:9
  978.3 2.3 slice_select_fusion
  980.6 60.2 %all-reduce.11.cloned.1.call-done = f32[512,512]{0,1:T(8,128)} async-done(((f32[512,512]{0,1:T(8,128)}), f32[512,512]{0,1:T(8,128)}) %all-reduce.11.cloned.1.call-update) | async-done | bytes 1048592 | tf_op jit(solution)/shard_map/psum | solution.py:9
  1040.8 21.8 %subtract_select_fusion = f32[512,4096]{0,1:T(8,128)} fusion(f32[512,4096]{0,1:T(8,128)} %all-reduce.9.cloned.1.call-done, f32[512,4096]{0,1:T(8,128)} %get-tuple-element.48, f32[512,512]{0,1:T(8,128)} %all-reduce.11.cloned.1.call-done, pred[]{:T(512)S(6)} %eq.24), kind=kOutput, calls=%fused_computation.13 | convolution fusion | flops 12889096192 | bytes 26214400 | tf_op jit(solution)/shard_map/dot_general | solution.py:43
  1062.6 10.4 copy.20
  (82 shorter events, 27.5 us)
Async XLA Ops:
  6.5 213.7 %all-reduce.13.cloned.1.call-start = ((), (), s32[]{:S(2)}) async-start(), calls=%async_computation.5 | async-start | bytes 16777216 | tf_op jit(solution)/shard_map/psum | solution.py:9
  41.7 178.5 %copy-start.6 = (f32[2048]{0:T(1024)S(1)}, f32[2048]{0:T(1024)}, u32[]{:S(2)}) copy-start(f32[2048]{0:T(1024)} %param.7) | copy-start | bytes 24580
  41.7 511.2 %reduce-scatter.2.cloned.1.call-start = ((), (), s32[]{:S(2)}) async-start(), calls=%async_computation.1 | async-start | bytes 41943040 | tf_op jit(solution)/shard_map/reduce_scatter | solution.py:29
  264.1 288.8 %copy-start.5 = (f32[512]{0:T(512)S(1)}, f32[512]{0:T(512)}, u32[]{:S(2)}) copy-start(f32[512]{0:T(512)} %param.9) | copy-start | bytes 6148
  264.1 351.7 %all-reduce.7.cloned.1.call-start = ((), (), s32[]{:S(2)}) async-start(), calls=%async_computation.2 | async-start | bytes 2097152 | tf_op jit(solution)/shard_map/psum | solution.py:9
  556.3 422.0 %all-reduce.9.cloned.1.call-start = ((), (), s32[]{:S(2)}) async-start(), calls=%async_computation.3 | async-start | bytes 16777216 | tf_op jit(solution)/shard_map/psum | solution.py:9
  615.8 1.7 copy-start.4
  764.6 11.7 %copy-start = (f32[128,4096]{1,0:T(8,128)}, f32[128,4096]{1,0:T(8,128)S(1)}, u32[]{:S(2)}) copy-start(f32[128,4096]{1,0:T(8,128)S(1)} %fusion.37) | copy-start | bytes 6291460
  776.2 1.3 copy-start.1
  798.1 3.5 copy-start.2
  798.1 3.5 copy-start.3
  807.1 233.7 %all-reduce.11.cloned.1.call-start = ((), (), s32[]{:S(2)}) async-start(), calls=%async_computation.4 | async-start | bytes 2097152 | tf_op jit(solution)/shard_map/psum | solution.py:9
Sparse Core Ops, SparseCore 0:
  41.9 178.3 all-reduce.12
  264.2 288.6 reduce-scatter.1
  556.4 59.2 all-reduce.6
  807.2 171.0 all-reduce.8
  980.7 60.0 all-reduce.10
where the time goes:
time: 1080 us
  waiting for transfers between devices  757 us (70%)
  other arithmetic  146 us (14%)
  matrix products  107 us (10%)
  local copies, waits for them, and re-layouts  53.1 us (5%)
  between operations  16.3 us (2%)
    psum x4, waiting for transfers between devices, spread(): return lax.psum(jnp.where(mine, value, jnp.zeros_like(value)), axis)  469 us
    reduce_scatter x1, waiting for transfers between devices, body(): lax.psum_scatter(jnp.einsum('sb,sc->bc', band, weighted, preferred_elemen...  288 us
    another operation x14, other arithmetic, body(): lower = jnp.linalg.cholesky(corner)  79 us
    dot_general x1, matrix products, body(): jnp.einsum('sb,sc->bc', band, weighted, preferred_element_type=jnp.float32)  43.8 us
    another operation x3, other arithmetic, body(): local_solved = jax.scipy.linalg.solve_triangular(lower, fisher, lower=True)  40.3 us
    another operation x7, matrix products, body(): local_solved = jax.scipy.linalg.solve_triangular(lower, fisher, lower=True)  38.7 us
    dot_general x1, matrix products, body(): jnp.dot(solved_mine.T, solved, precision=lax.Precision.HIGHEST)  21.8 us
  transfers between devices with their start and end apart: 5, of which 5 were waited for; matrix products, arithmetic and copies ran while one was open for 0% of the time, Pallas kernels for 0%

commit v1 on v0

--- a/solution.py
+++ b/solution.py
@@ -26,22 +26,41 @@
     for owner in range(row_count):
         band_parts.append(spread(first_tile, "col", owner))
     band = jnp.concatenate(band_parts, axis=1)
-    fisher = lax.psum_scatter(
-        jnp.einsum("sb,sc->bc", band, weighted, preferred_element_type=jnp.float32),
+    band_weighted = (sample_weight[:, None] * band.astype(jnp.float32)).astype(jnp.bfloat16)
+
+    head = lax.psum(
+        jnp.einsum("sb,sc->bc", band[:, :tile], band_weighted, preferred_element_type=jnp.float32),
         "row",
-        scatter_dimension=0,
-        tiled=True,
     )
-    on_diagonal = (lax.axis_index("col") == lax.axis_index("row")).astype(jnp.float32)
+    prior_head = lax.all_gather(prior, "row", tiled=True)[:tile]
     identity = jnp.eye(tile, dtype=jnp.float32)
-    fisher = fisher.at[:, :tile].add(on_diagonal * identity * prior[None, :])
-    corner = spread(fisher[:, :tile], "col", 0)
+    corner = head[:, :tile] + identity * prior_head[None, :]
     lower = jnp.linalg.cholesky(corner)
-    local_solved = jax.scipy.linalg.solve_triangular(lower, fisher, lower=True)
-    solved = spread(local_solved, "row", 0)
-    solved_mine = spread(solved[:, :tile], "col", lax.axis_index("row"))
-    updated = fisher - jnp.dot(solved_mine.T, solved, precision=lax.Precision.HIGHEST)
-    result = jnp.where(lax.axis_index("row") == 0, solved, updated)
+    lower_inv = jax.scipy.linalg.solve_triangular(lower, identity, lower=True)
+    hi = lax.Precision.HIGHEST
+    side_panel = jnp.dot(lower_inv, head[:, tile:], precision=hi)
+    side_t = jnp.dot(side_panel.T, lower_inv, precision=hi)
+    transform = jnp.concatenate([lower_inv, -side_t], axis=0)
+
+    part_head = jnp.einsum(
+        "sb,sc->bc", band[:, :tile], weighted, preferred_element_type=jnp.float32
+    )
+    part_rest = jnp.einsum(
+        "sb,sc->bc", band[:, tile:], weighted, preferred_element_type=jnp.float32
+    )
+    moved = jnp.dot(transform, part_head, precision=lax.Precision.HIGH)
+    partial = moved + jnp.concatenate(
+        [jnp.zeros((tile, widths), jnp.float32), part_rest], axis=0
+    )
+    result = lax.psum_scatter(partial, "row", scatter_dimension=0, tiled=True)
+
+    row = lax.axis_index("row")
+    col = lax.axis_index("col")
+    mine = lax.dynamic_slice_in_dim(transform, row * tile, tile, axis=0)
+    head_on = (col == 0).astype(jnp.float32)
+    diag_on = ((col == row) & (row != 0)).astype(jnp.float32)
+    fix = head_on * mine * prior_head[None, :] + diag_on * identity * prior[None, :]
+    result = result.at[:, :tile].add(fix)
     return result.reshape(tile, cycles, tile)
 
 

time: 1080 us -> 853 us (0.79)
  waiting for transfers between devices: 757 us -> 510 us
  matrix products: 107 us -> 122 us
    psum x4 -> x1, waiting for transfers between devices: 469 us -> 168 us  [spread(): return lax.psum(jnp.where(mine, value, jnp.zeros_like(value)), axis)]
    psum x0 -> x1, waiting for transfers between devices: none -> 53.8 us  [body(): lax.psum(jnp.einsum('sb,sc->bc', band[:, :tile], band_weighted, preferred...]
    dot_general x2 -> x6, matrix products: 65.6 us -> 112 us  [the longest x1 34.8 us: body(): moved = jnp.dot(transform, part_head, precision=lax.Precision.HIGH)]
    another operation x7, matrix products: 38.7 us -> 6.3 us  [body(): lower_inv = jax.scipy.linalg.solve_triangular(lower, identity, lower=True)]
    select_n x4 -> x1, other arithmetic: 16.1 us -> 5.07 us  [spread(): return lax.psum(jnp.where(mine, value, jnp.zeros_like(value)), axis)]
  transfers between devices with their start and end apart: 5 -> 3, of which waited for: 5 -> 3; matrix products, arithmetic and copies ran while one was open for 0% -> 6% of each run, Pallas kernels for 0% -> 0%
where the time goes in v1:
time: 853 us; the launch traced here: 846 us
  waiting for transfers between devices  510 us (60%)
  other arithmetic  141 us (17%)
  matrix products  122 us (14%)
  local copies, waits for them, and re-layouts  46.3 us (5%)
  between operations  16.2 us (2%)
  blocking collectives  9.56 us (1%)
    reduce_scatter x1, waiting for transfers between devices, body(): result = lax.psum_scatter(partial, 'row', scatter_dimension=0, tiled=True)  288 us
    psum x1, waiting for transfers between devices, spread(): return lax.psum(jnp.where(mine, value, jnp.zeros_like(value)), axis)  168 us
    another operation x14, other arithmetic, body(): lower = jnp.linalg.cholesky(corner)  79 us
    psum x1, waiting for transfers between devices, body(): lax.psum(jnp.einsum('sb,sc->bc', band[:, :tile], band_weighted, preferred...  53.8 us
    another operation x3, other arithmetic, body(): lower_inv = jax.scipy.linalg.solve_triangular(lower, identity, lower=True)  40.3 us
    dot_general x1, matrix products, body(): moved = jnp.dot(transform, part_head, precision=lax.Precision.HIGH)  34.8 us
    dot_general x1, matrix products, body(): jnp.einsum('sb,sc->bc', band[:, tile:], weighted, preferred_element_type=...  34.1 us
    unnamed x17, local copies, waits for them, and re-layouts  22 us
  transfers between devices with their start and end apart: 3, of which 3 were waited for; matrix products, arithmetic and copies ran while one was open for 6% of the time, Pallas kernels for 0%

profile of v1, /device:TPU:0, one launch (start us, length us, event | category | flops | bytes accessed | tf_op | source)
XLA Modules:
  0.0 846.1 jit_solution(15876469855539642256)
XLA Ops:
  7.2 1.7 mul.67
  9.0 6.3 copy.50
  15.2 12.2 %copy.49 = bf16[256,8,8,512]{3,1,2,0:T(8,128)(2,1)S(1)} copy(bf16[256,8,8,512]{3,2,1,0:T(8,128)(2,1)} %bitcast.65) | data formatting | bytes 33554432
  27.4 9.4 %mul.69 = bf16[2048,4096]{1,0:T(8,128)(2,1)} multiply(bf16[2048,4096]{1,0:T(8,128)(2,1)S(1)} %bitcast.63, bf16[2048,4096]{1,0:T(8,128)(2,1)S(1)} %bitcast.62) | non-fusion elementwise | flops 8388608 | bytes 50331648 | tf_op jit(solution)/shard_map/mul | solution.py:19
  36.8 5.1 broadcast_select_fusion.3
  42.5 9.6 %all-gather = f32[4,1,512]{2,1,0:T(1,128)S(1)} all-gather(f32[1,1,512]{2,1,0:T(1,128)S(1)} %bitcast.70), channel_id=1, replica_groups=mesh['row'=4,'col'=8] {'row'}, dimensions={0}, use_global_device_ids=true | all-gather | bytes 10240 | tf_op jit(solution)/shard_map/all_gather | solution.py:35
  52.3 168.0 %all-reduce.8.cloned.1.call-done = (bf16[2048,512]{1,0:T(8,128)(2,1)}, bf16[2048,512]{1,0:T(8,128)(2,1)}, bf16[2048,512]{1,0:T(8,128)(2,1)}, bf16[2048,512]{1,0:T(8,128)(2,1)}) async-done(((bf16[2048,512]{1,0:T(8,128)(2,1)}, bf16[2048,512]{1,0:T(8,128)(2,1)}, bf16[2048,512]{1,0:T(8,128)(2,1)}, bf16[2048,512]{1,0:T(8,128)(2,1)}), (bf16[2048,512]{1,0:T(8,128)(2,1)}, bf16[2048,512]{1,0:T(8,128)(2,1)}, ...) | async-done | bytes 8388624 | tf_op jit(solution)/shard_map/psum | solution.py:9
  220.3 12.8 %fusion = f32[512,2048]{0,1:T(8,128)} fusion(bf16[2048,512]{1,0:T(8,128)(2,1)} %get-tuple-element.44, bf16[2048,512]{1,0:T(8,128)(2,1)} %get-tuple-element.41, bf16[2048,512]{1,0:T(8,128)(2,1)} %get-tuple-element.42, bf16[2048,512]{1,0:T(8,128)(2,1)} %get-tuple-element.43, f32[2048]{0:T(1024)S(1)} %copy-done.4), kind=kOutput, calls=%fused_computation.5 | convolution fusion | flops 4336910336 | bytes 12591104 | tf_op jit(solution)/shard_map/sb,sc->bc/dot_general | solution.py:32
  233.4 34.1 %fusion.9 = f32[1536,4096]{0,1:T(8,128)} fusion(bf16[2048,4096]{1,0:T(8,128)(2,1)} %mul.69, f32[2048]{0:T(1024)S(1)} %copy-done.4, bf16[2048,512]{1,0:T(8,128)(2,1)} %get-tuple-element.41, bf16[2048,512]{1,0:T(8,128)(2,1)} %get-tuple-element.42, bf16[2048,512]{1,0:T(8,128)(2,1)} %get-tuple-element.43), kind=kOutput, calls=%fused_computation.14 | convolution fusion | flops 25813843968 | bytes 48242688 | tf_op jit(solution)/shard_map/sb,sc->bc/dot_general | solution.py:48
  267.5 15.8 %fusion.10 = f32[512,4096]{1,0:T(8,128)} fusion(bf16[2048,512]{1,0:T(8,128)(2,1)S(1)} %copy-done.3, bf16[2048,4096]{1,0:T(8,128)(2,1)} %mul.69, f32[2048]{0:T(1024)S(1)} %copy-done.4), kind=kOutput, calls=%fused_computation.15 | convolution fusion | flops 8615100416 | bytes 27271168 | tf_op jit(solution)/shard_map/sb,sc->bc/dot_general | solution.py:45
  283.2 53.8 %all-reduce.6.cloned.1.call-done = f32[512,2048]{0,1:T(8,128)} async-done(((f32[512,2048]{0,1:T(8,128)}), f32[512,2048]{0,1:T(8,128)}) %all-reduce.6.cloned.1.call-update) | async-done | bytes 4194320 | tf_op jit(solution)/shard_map/psum | solution.py:31
  337.0 1.4 slice_add_fusion
  338.8 1.5 fusion.20
  340.3 11.7 %cholesky.103 = f32[128,128]{1,0:T(8,128)S(1)} custom-call(f32[128,128]{1,0:T(8,128)S(1)} %cholesky.263), custom_call_target="Cholesky" | custom-call | tf_op jit(solution)/shard_map/jit(cholesky)/cholesky | solution.py:38
  352.0 9.8 %custom-call.31 = f32[1,128,128]{1,2,0:T(8,128)S(1)} custom-call(f32[1,128,128]{2,1,0:T(8,128)S(1)} %get-tuple-element.56), custom_call_target="InvertDiagBlocksLowerTriangular" | custom-call | tf_op jit(solution)/shard_map/jit(cholesky)/cholesky | solution.py:38
  362.5 11.7 %cholesky.215 = f32[128,128]{1,0:T(8,128)S(1)} custom-call(f32[128,128]{1,0:T(8,128)S(1)} %cholesky.267), custom_call_target="Cholesky" | custom-call | tf_op jit(solution)/shard_map/jit(cholesky)/cholesky | solution.py:38
  374.6 10.2 %custom-call.32 = f32[1,128,128]{1,2,0:T(8,128)S(1)} custom-call(f32[1,128,128]{2,1,0:T(8,128)S(1)} %get-tuple-element.54), custom_call_target="InvertDiagBlocksLowerTriangular" | custom-call | tf_op jit(solution)/shard_map/jit(cholesky)/cholesky | solution.py:38
  385.3 1.5 convolution_subtract_fusion.4
  386.9 11.7 %cholesky.236 = f32[128,128]{1,0:T(8,128)S(1)} custom-call(f32[128,128]{1,0:T(8,128)S(1)} %cholesky.272), custom_call_target="Cholesky" | custom-call | tf_op jit(solution)/shard_map/jit(cholesky)/cholesky | solution.py:38
  398.7 9.8 %custom-call.33 = f32[1,128,128]{1,2,0:T(8,128)S(1)} custom-call(f32[1,128,128]{2,1,0:T(8,128)S(1)} %get-tuple-element.52), custom_call_target="InvertDiagBlocksLowerTriangular" | custom-call | tf_op jit(solution)/shard_map/jit(cholesky)/cholesky | solution.py:38
  408.8 1.3 convolution_subtract_fusion.5
  410.2 11.9 %cholesky.253 = f32[128,128]{1,0:T(8,128)S(1)} custom-call(f32[128,128]{1,0:T(8,128)S(1)} %convolution_subtract_fusion.5), custom_call_target="Cholesky" | custom-call | tf_op jit(solution)/shard_map/jit(cholesky)/cholesky | solution.py:38
  426.8 10.7 %while.2 = (s32[]{:T(128)}, f32[512,512]{0,1:T(8,128)S(1)}, s32[4,2]{0,1:T(2,128)S(1)}, f32[4,128,128]{2,1,0:T(8,128)}, s32[]{:T(128)}) while((s32[]{:T(128)}, f32[512,512]{0,1:T(8,128)S(1)}, s32[4,2]{0,1:T(2,128)S(1)}, f32[4,128,128]{2,1,0:T(8,128)}, s32[]{:T(128)}) %tuple.32), condition=%wide.while_cond.1, body=%wide.while_body.1.sunk | while | flops 2 | bytes 393829 | solution.py:39
  430.1 1.3 dynamic-slice.15
  437.5 40.1 %custom-call.34 = f32[4,128,128]{1,2,0:T(8,128)S(1)} custom-call(f32[4,128,128]{2,1,0:T(8,128)} %get-tuple-element.24), custom_call_target="InvertDiagBlocksLowerTriangular" | custom-call | tf_op jit(solution)/shard_map/jit(_solve_triangular)/triangular_solve | solution.py:39
  481.3 1.5 convolution_subtract_fusion.2
  487.5 7.3 fusion.17
  494.8 7.2 fusion.16
  502.0 34.8 %pad_add_fusion = f32[2048,4096]{0,1:T(8,128)} fusion(f32[1536,4096]{0,1:T(8,128)} %fusion.9, f32[2048,512]{0,1:T(8,128)} %fusion.16, f32[512,4096]{1,0:T(8,128)} %fusion.10), kind=kOutput, calls=%fused_computation.2 | convolution fusion | flops 25778192384 | bytes 71303168 | tf_op jit(solution)/shard_map/dot_general | solution.py:51
  537.5 288.0 %reduce-scatter.2.cloned.1.call-done = f32[512,4096]{0,1:T(8,128)} async-done(((f32[2048,4096]{0,1:T(8,128)}), f32[512,4096]{0,1:T(8,128)}) %reduce-scatter.2.cloned.1.call-update) | async-done | bytes 8388624 | tf_op jit(solution)/shard_map/reduce_scatter | solution.py:55
  825.5 3.4 fusion.19
  828.9 10.4 %copy.40 = f32[512,8,512]{2,1,0:T(8,128)} copy(f32[512,8,512]{0,2,1:T(8,128)} %bitcast.66) | data formatting | bytes 16777216 | tf_op jit(solution)/shard_map/reshape | solution.py:64
  (84 shorter events, 24.7 us)
Async XLA Ops:
  6.5 213.8 %all-reduce.8.cloned.1.call-start = ((), (), s32[]{:S(2)}) async-start(), calls=%async_computation.3 | async-start | bytes 16777216 | tf_op jit(solution)/shard_map/psum | solution.py:9
  41.8 0.7 copy-start.2
  41.8 178.5 %copy-start.4 = (f32[2048]{0:T(1024)S(1)}, f32[2048]{0:T(1024)}, u32[]{:S(2)}) copy-start(f32[2048]{0:T(1024)} %param.7) | copy-start | bytes 24580
  41.9 295.2 %all-reduce.6.cloned.1.call-start = ((), (), s32[]{:S(2)}) async-start(), calls=%async_computation.1 | async-start | bytes 8388608 | tf_op jit(solution)/shard_map/psum | solution.py:31
  233.2 34.3 %copy-start.3 = (bf16[2048,512]{1,0:T(8,128)(2,1)S(1)}, bf16[2048,512]{1,0:T(8,128)(2,1)}, u32[]{:S(2)}) copy-start(bf16[2048,512]{1,0:T(8,128)(2,1)} %get-tuple-element.44) | copy-start | bytes 6291460
  233.2 592.3 %reduce-scatter.2.cloned.1.call-start = ((), (), s32[]{:S(2)}) async-start(), calls=%async_computation.2 | async-start | bytes 41943040 | tf_op jit(solution)/shard_map/reduce_scatter | solution.py:55
  340.3 34.4 %copy-start = (f32[512,512]{1,0:T(8,128)}, f32[512,512]{1,0:T(8,128)S(1)}, u32[]{:S(2)}) copy-start(f32[512,512]{1,0:T(8,128)S(1)} %fusion.20) | copy-start | bytes 3145732
  477.6 0.9 copy-start.1
Sparse Core Ops, SparseCore 0:
  42.0 178.3 all-reduce.7
  233.3 103.7 all-reduce.5
  536.9 288.5 reduce-scatter.1
